TPU v7x, 256 devices: a whole 4x4x8 slice. The times are simulated.
256 devices in a mesh: ctx: 64 (over z, y_hi, x), head: 4 (over y_lo, core).
Axes of the slice: x: 4, y: 4 (y_hi: 2, y_lo: 2; y = y_hi * 2 + y_lo), z: 8, core: 2. Of those that a mesh axis runs over, the one named last changes fastest.
Arguments:
- query_rows: bfloat16 [32768, 5120], P(('ctx', 'head')), may hold values from -6 to 6
- key_rows: bfloat16 [32768, 1024], P(('ctx', 'head')), may hold values from -6 to 6
- value_rows: bfloat16 [32768, 1024], P(('ctx', 'head')), may hold values from -6 to 6
- attn_output: bfloat16 [32768, 5120], P(('ctx', 'head')), may hold values from -3 to 3
- out_grad: bfloat16 [32768, 5120], P(('ctx', 'head')), may hold values from -24 to 24
- log_norm: float32 [40, 32768], P('head', 'ctx'), may hold values from 5 to 7
- prefix_keys: bfloat16 [1024, 1024], P('ctx', 'head'), may hold values from -6 to 6
- prefix_values: bfloat16 [1024, 1024], P('ctx', 'head'), may hold values from -6 to 6
- response_blocks: int32 [128], replicated, may hold values from 1 to 16, as said below
- prompt_members: int32 [8, 16], replicated, may hold values from 0 to 127, as said below
Outputs:
- query_grad: bfloat16 [32768, 5120], P('ctx', 'head')
- key_grad: bfloat16 [32768, 1024], P('ctx', 'head')
- value_grad: bfloat16 [32768, 1024], P('ctx', 'head')
- prefix_keygrads: bfloat16 [1024, 1024], P('ctx', 'head')
- prefix_valuegrads: bfloat16 [1024, 1024], P('ctx', 'head')
Inputs may be any that keep to these rules, and one draw needn't show every extreme that they name: `response_blocks`: the lengths fill all 1024 blocks of the row. Every index of ctx from 1 on begins inside a response that started on the index before it. `prompt_members`: every response, numbered 0 to 127 in order along the row, is listed exactly once.
All inputs are finite; a program needn't handle non-finite values.
Results may differ from a plain program's by a relative error of at most 0.008.
Values may be sent and summed in bfloat16 or wider, within the bound.
No kernel may reach another device: no remote copies, remote signals or barrier semaphores. Data moves between devices by JAX's collectives and lax.ppermute only.
A program may use at most 64 MiB of HBM per device.

v0:
```python
import math
import jax
import jax.numpy as jnp
from jax import lax
from jax.sharding import PartitionSpec as P

HD = 128
BLK = 32
PL = 128


def shifted(array, axis, by):
    devices = lax.axis_size(axis)
    pairs = [(i, i + by) for i in range(devices) if 0 <= i + by < devices]
    return lax.ppermute(array, axis, pairs)


def token_tables(response_blocks, prompt_members, first_block, count):
    starts = jnp.cumsum(response_blocks) - response_blocks
    responses = response_blocks.shape[0]
    group = prompt_members.shape[1]
    listed = prompt_members.reshape(-1)
    owner = jnp.arange(listed.shape[0], dtype=jnp.int32) // group
    numbers = jnp.arange(responses, dtype=jnp.int32)
    hits = listed[:, None] == numbers[None, :]
    prompt_of = jnp.sum(jnp.where(hits, owner[:, None], 0), axis=0)
    blocks = first_block + jnp.arange(count, dtype=jnp.int32)
    before = starts[None, :] <= blocks[:, None]
    first = jnp.max(jnp.where(before, starts[None, :], 0), axis=1)
    current = jnp.sum(before.astype(jnp.int32), axis=1) - 1
    chosen = numbers[None, :] == current[:, None]
    prompt_block = jnp.sum(jnp.where(chosen, prompt_of[None, :], 0), axis=1)
    return (jnp.repeat(first * BLK, BLK), jnp.repeat(prompt_block, BLK))


def tile_terms(queries, grads, norms, deltas, keys, values, allowed):
    rows = queries.shape[0]
    cols = keys.shape[0]
    heads = norms.shape[1]
    group = heads // (keys.shape[1] // HD)
    scale = 1.0 / math.sqrt(HD)

    def one_head(head, carry):
        query_acc, key_acc, value_acc = carry
        kv_head = head // group
        query_h = lax.dynamic_slice_in_dim(queries, head * HD, HD, 1)
        grad_h = lax.dynamic_slice_in_dim(grads, head * HD, HD, 1)
        key_h = lax.dynamic_slice_in_dim(keys, kv_head * HD, HD, 1)
        value_h = lax.dynamic_slice_in_dim(values, kv_head * HD, HD, 1)
        norm_h = lax.dynamic_slice_in_dim(norms, head, 1, 1)
        delta_h = lax.dynamic_slice_in_dim(deltas, head, 1, 1)
        logits = jnp.dot(query_h, key_h.T, preferred_element_type=jnp.float32)
        weights = jnp.where(allowed, jnp.exp(logits * scale - norm_h), 0.0)
        weights_b = weights.astype(jnp.bfloat16)
        value_term = jnp.dot(weights_b.T, grad_h, preferred_element_type=jnp.float32)
        dweights = jnp.dot(grad_h, value_h.T, preferred_element_type=jnp.float32)
        dlogits = (weights * (dweights - delta_h)).astype(jnp.bfloat16)
        query_term = jnp.dot(dlogits, key_h, preferred_element_type=jnp.float32)
        key_term = jnp.dot(dlogits.T, query_h, preferred_element_type=jnp.float32)
        query_acc = lax.dynamic_update_slice_in_dim(query_acc, query_term, head * HD, 1)
        old_key = lax.dynamic_slice_in_dim(key_acc, kv_head * HD, HD, 1)
        key_acc = lax.dynamic_update_slice_in_dim(key_acc, old_key + key_term, kv_head * HD, 1)
        old_value = lax.dynamic_slice_in_dim(value_acc, kv_head * HD, HD, 1)
        value_acc = lax.dynamic_update_slice_in_dim(
            value_acc, old_value + value_term, kv_head * HD, 1
        )
        return (query_acc, key_acc, value_acc)

    start = (
        jnp.zeros((rows, queries.shape[1]), jnp.float32),
        jnp.zeros((cols, keys.shape[1]), jnp.float32),
        jnp.zeros((cols, keys.shape[1]), jnp.float32),
    )
    return lax.fori_loop(0, heads, one_head, start)


def add_rows(total, term, offset):
    old = lax.dynamic_slice_in_dim(total, offset, term.shape[0], 0)
    return lax.dynamic_update_slice_in_dim(total, old + term, offset, 0)


def shards(
    query_rows,
    key_rows,
    value_rows,
    attn_output,
    out_grad,
    log_norm,
    prefix_keys,
    prefix_values,
    response_blocks,
    prompt_members,
):
    queries, keys, values, outputs, grads = (
        lax.all_to_all(query_rows, "head", split_axis=1, concat_axis=0, tiled=True),
        lax.all_to_all(key_rows, "head", split_axis=1, concat_axis=0, tiled=True),
        lax.all_to_all(value_rows, "head", split_axis=1, concat_axis=0, tiled=True),
        lax.all_to_all(attn_output, "head", split_axis=1, concat_axis=0, tiled=True),
        lax.all_to_all(out_grad, "head", split_axis=1, concat_axis=0, tiled=True),
    )
    own_heads = queries.shape[1] // HD
    deltas = jnp.einsum(
        "thd,thd->th",
        grads.reshape(-1, own_heads, HD),
        outputs.reshape(-1, own_heads, HD),
        preferred_element_type=jnp.float32,
    )
    tokens = queries.shape[0]
    scale = 1.0 / math.sqrt(HD)
    norms = log_norm.T
    position = lax.axis_index("ctx")
    base = position * tokens
    starts, prompts = token_tables(
        response_blocks, prompt_members, position * (tokens // BLK), tokens // BLK
    )
    local_start = starts - base
    positions = jnp.arange(tokens, dtype=jnp.int32)
    allowed_here = (positions[None, :] >= local_start[:, None]) & (
        positions[None, :] <= positions[:, None]
    )
    allowed_prior = positions[None, :] - tokens >= local_start[:, None]
    query_one, key_one, value_one = tile_terms(
        queries, grads, norms, deltas, keys, values, allowed_here
    )
    keys_prior, values_prior = shifted((keys, values), "ctx", 1)
    query_two, key_two, value_two = tile_terms(
        queries, grads, norms, deltas, keys_prior, values_prior, allowed_prior
    )
    back_keys, back_values = (
        shifted(key_two.astype(jnp.bfloat16), "ctx", -1).astype(key_two.dtype),
        shifted(value_two.astype(jnp.bfloat16), "ctx", -1).astype(value_two.dtype),
    )
    whole_keys, whole_values = (
        lax.all_gather(prefix_keys, "ctx", axis=0, tiled=True),
        lax.all_gather(prefix_values, "ctx", axis=0, tiled=True),
    )
    prompt_total = whole_keys.shape[0]
    prompt_count = prompt_total // PL
    width = prefix_keys.shape[1]
    init = (
        query_one + query_two,
        jnp.zeros((prompt_total, width), jnp.float32),
        jnp.zeros((prompt_total, width), jnp.float32),
    )

    def prompt_step(number, state):
        seen = prompts == number

        def compute(inner):
            total, pkeys, pvalues = inner
            keys_p = lax.dynamic_slice_in_dim(whole_keys, number * PL, PL, 0)
            values_p = lax.dynamic_slice_in_dim(whole_values, number * PL, PL, 0)
            allowed = jnp.broadcast_to(seen[:, None], (tokens, PL))
            query_p, key_p, value_p = tile_terms(
                queries, grads, norms, deltas, keys_p, values_p, allowed
            )
            return (
                total + query_p,
                add_rows(pkeys, key_p, number * PL),
                add_rows(pvalues, value_p, number * PL),
            )

        return lax.cond(jnp.any(seen), compute, lambda inner: inner, state)

    query_total, pkey_acc, pvalue_acc = lax.fori_loop(0, prompt_count, prompt_step, init)
    pkey_sum, pvalue_sum = (
        lax.psum_scatter(pkey_acc, "ctx", scatter_dimension=0, tiled=True),
        lax.psum_scatter(pvalue_acc, "ctx", scatter_dimension=0, tiled=True),
    )
    return (
        (query_total * scale).astype(jnp.bfloat16),
        ((key_one + back_keys) * scale).astype(jnp.bfloat16),
        (value_one + back_values).astype(jnp.bfloat16),
        (pkey_sum * scale).astype(jnp.bfloat16),
        pvalue_sum.astype(jnp.bfloat16),
    )


def solution(mesh):
    placed = (
        P(("ctx", "head"), None),
        P(("ctx", "head"), None),
        P(("ctx", "head"), None),
        P(("ctx", "head"), None),
        P(("ctx", "head"), None),
        P("head", "ctx"),
        P("ctx", "head"),
        P("ctx", "head"),
        P(),
        P(),
    )
    return jax.shard_map(
        shards,
        mesh=mesh,
        in_specs=placed,
        out_specs=(
            P("ctx", "head"),
            P("ctx", "head"),
            P("ctx", "head"),
            P("ctx", "head"),
            P("ctx", "head"),
        ),
        check_vma=False,
    )
```

profile of v0, /device:TPU:8, one launch (start us, length us, event | category | flops | bytes accessed | tf_op | source)
XLA Modules:
  0.0 1574.4 jit_solution(12429472949831046137)
XLA Ops:
  8.9 5.5 all-to-all-start.1
  16.2 2.7 all-to-all-done.1
  18.9 5.0 all-to-all-start.3
  25.3 2.9 all-to-all-done.3
  28.2 5.3 all-to-all-start.2
  35.0 14.1 all-to-all-done.2
  49.1 5.3 all-to-all-start.4
  54.8 2.5 copy.65
  57.7 12.3 all-to-all-done.4
  70.0 6.1 all-to-all-start
  76.3 195.1 %all_gather.6 = bf16[1024,256]{1,0:T(8,128)(2,1)} all-gather(bf16[16,256]{1,0:T(8,128)(2,1)S(1)} %copy-done.9), channel_id=1, replica_groups=mesh['ctx'=64,'head'=4] {'ctx'}, dimensions={0}, use_global_device_ids=true | all-gather | bytes 532480 | tf_op jit(solution)/shard_map/all_gather | solution.py:134
  271.4 186.6 %all_gather.7 = bf16[1024,256]{1,0:T(8,128)(2,1)} all-gather(bf16[16,256]{1,0:T(8,128)(2,1)S(1)} %copy-done.10), channel_id=1, replica_groups=mesh['ctx'=64,'head'=4] {'ctx'}, dimensions={0}, use_global_device_ids=true | all-gather | bytes 532480 | tf_op jit(solution)/shard_map/all_gather | solution.py:135
  458.1 3.9 collective-permute-start
  462.0 2.6 collective-permute-start.1
  464.7 6.9 copy.49
  471.7 3.5 reshape.101
  475.2 6.9 copy.51
  482.1 3.5 reshape.102
  491.1 69.6 %while.79 = (s32[]{:T(128)}, f32[512,1280]{1,0:T(8,128)}, f32[512,256]{1,0:T(8,128)S(1)}, f32[512,256]{1,0:T(8,128)S(1)}, bf16[512,1280]{1,0:T(8,128)(2,1)}, /*i...) while((s32[]{:T(128)}, f32[512,1280]{1,0:T(8,128)}, ...), condition=%wide.region_5.6_spmd.clone, body=%wide.region_4.5_spmd.clone.sunk | while | flops 337772544 | bytes 6963587 | solution.py:74
  562.5 69.3 %while.78 = (s32[]{:T(128)}, f32[512,1280]{1,0:T(8,128)}, f32[512,256]{1,0:T(8,128)S(1)}, f32[512,256]{1,0:T(8,128)S(1)}, bf16[512,1280]{1,0:T(8,128)(2,1)}, /*i...) while((s32[]{:T(128)}, f32[512,1280]{1,0:T(8,128)}, ...), condition=%wide.region_3.4_spmd.clone, body=%wide.region_2.3_spmd.clone.sunk | while | flops 338296832 | bytes 6961531 | solution.py:74
  631.8 4.7 add.320
  638.6 136.6 %while.80 = (s32[]{:T(128)}, f32[512,1280]{1,0:T(8,128)}, f32[1024,256]{1,0:T(8,128)}, f32[1024,256]{1,0:T(8,128)}, bf16[1024,256]{1,0:T(8,128)(2,1)}, /*index=5...) while((s32[]{:T(128)}, f32[512,1280]{1,0:T(8,128)}, ...), condition=%wide.region_15.16_spmd.clone, body=%wide.region_9.15_spmd.clone.sunk | while | flops 85099536 | bytes 14145448 | solution.py:165
  640.0 62.4 %conditional.3 = ((f32[512,1280]{1,0:T(8,128)}, f32[1024,256]{1,0:T(8,128)}, f32[1024,256]{1,0:T(8,128)})) conditional(s32[]{:T(128)} %convert_element_type.143, (f32[512,1280]{1,0:T(8,128)}, f32[1024,256]{1,0:T(8,128)}, f32[1024,256]{1,0:T(8,128)}) %tuple.159, (s32[]{:T(128)}, bf16[1024,256]{1,0:T(8,128)(2,1)}, bf16[1024,256]{1,0:T(8,128)(2,1)}, ...), branch_computations={%region_11.11_spmd, %region_12.14_spmd} | conditional | flops 85098512 | bytes 14136441 | solution.py:163
  641.9 55.2 %while.77 = (s32[]{:T(128)}, f32[512,1280]{1,0:T(8,128)S(1)}, f32[128,256]{1,0:T(8,128)S(1)}, f32[128,256]{1,0:T(8,128)S(1)}, bf16[512,1280]{1,0:T(8,128)(2,1)},...) while((s32[]{:T(128)}, f32[512,1280]{1,0:T(8,128)S(1)}, ...), condition=%wide.region_14.13_spmd.clone, body=%wide.region_13.12_spmd.clone.sunk | while | flops 84377616 | bytes 2339707 | solution.py:74
  698.9 3.5 add.309
  711.3 62.4 %conditional.3 = ((f32[512,1280]{1,0:T(8,128)}, f32[1024,256]{1,0:T(8,128)}, f32[1024,256]{1,0:T(8,128)})) conditional(s32[]{:T(128)} %convert_element_type.143, (f32[512,1280]{1,0:T(8,128)}, f32[1024,256]{1,0:T(8,128)}, f32[1024,256]{1,0:T(8,128)}) %tuple.159, (s32[]{:T(128)}, bf16[1024,256]{1,0:T(8,128)(2,1)}, bf16[1024,256]{1,0:T(8,128)(2,1)}, ...), branch_computations={%region_11.11_spmd, %region_12.14_spmd} | conditional | flops 85098512 | bytes 14136441 | solution.py:163
  713.2 55.2 %while.77 = (s32[]{:T(128)}, f32[512,1280]{1,0:T(8,128)S(1)}, f32[128,256]{1,0:T(8,128)S(1)}, f32[128,256]{1,0:T(8,128)S(1)}, bf16[512,1280]{1,0:T(8,128)(2,1)},...) while((s32[]{:T(128)}, f32[512,1280]{1,0:T(8,128)S(1)}, ...), condition=%wide.region_14.13_spmd.clone, body=%wide.region_13.12_spmd.clone.sunk | while | flops 84377616 | bytes 2339707 | solution.py:74
  770.1 3.5 add.309
  778.9 3.1 multiply_convert_fusion
  781.9 2.6 collective-permute-done.3
  788.1 413.7 %reduce-scatter.5.cloned.1.call-done = f32[16,256]{1,0:T(8,128)} async-done(((f32[1024,256]{1,0:T(8,128)}), f32[16,256]{1,0:T(8,128)}) %reduce-scatter.5.cloned.1.call-update) | async-done | bytes 16400 | tf_op jit(solution)/shard_map/reduce_scatter | solution.py:168
  1203.1 363.1 %reduce-scatter.3.cloned.1.call-done = f32[16,256]{1,0:T(8,128)} async-done(((f32[1024,256]{1,0:T(8,128)}), f32[16,256]{1,0:T(8,128)}) %reduce-scatter.3.cloned.1.call-update) | async-done | bytes 16400 | tf_op jit(solution)/shard_map/reduce_scatter | solution.py:167
  (353 shorter events, 286.2 us)
Async XLA Ops:
  7.2 16.7 %copy-start.7 = (bf16[128,5120]{1,0:T(8,128)(2,1)S(1)}, bf16[128,5120]{1,0:T(8,128)(2,1)}, u32[]{:S(2)}) copy-start(bf16[128,5120]{1,0:T(8,128)(2,1)} %param.24) | copy-start | bytes 3932164
  8.9 9.9 all-to-all-start.1
  18.9 9.4 all-to-all-start.3
  28.2 5.3 copy-start.8
  28.2 20.9 %all-to-all-start.2 = ((bf16[128,4,1280]{0,2,1:T(8,128)(2,1)}), bf16[128,4,1280]{0,2,1:T(8,128)(2,1)S(1)}, u32[]{:S(2)}, u32[]{:S(2)}) async-start(bf16[128,4,1280]{0,2,1:T(8,128)(2,1)} %bitcast.5), calls=%async_computation.2 | async-start | bytes 2621440 | tf_op jit(solution)/shard_map/all_to_all | solution.py:99
  49.1 5.3 copy-start.12
  49.1 20.9 %all-to-all-start.4 = ((bf16[128,4,1280]{0,2,1:T(8,128)(2,1)}), bf16[128,4,1280]{0,2,1:T(8,128)(2,1)S(1)}, u32[]{:S(2)}, u32[]{:S(2)}) async-start(bf16[128,4,1280]{0,2,1:T(8,128)(2,1)} %bitcast.73), calls=%async_computation.4 | async-start | bytes 2621440 | tf_op jit(solution)/shard_map/all_to_all | solution.py:98
  54.8 2.5 copy-start.11
  70.0 6.2 copy-start.9
  70.0 201.4 %copy-start.10 = (bf16[16,256]{1,0:T(8,128)(2,1)S(1)}, bf16[16,256]{1,0:T(8,128)(2,1)}, u32[]{:S(2)}) copy-start(bf16[16,256]{1,0:T(8,128)(2,1)} %param.27) | copy-start | bytes 24580
  70.0 419.3 %all-to-all-start = ((bf16[128,4,1280]{2,0,1:T(8,128)(2,1)}), bf16[128,4,1280]{2,0,1:T(8,128)(2,1)}, u32[]{:S(2)}, u32[]{:S(2)}) async-start(bf16[128,4,1280]{2,0,1:T(8,128)(2,1)} %bitcast.72), calls=%async_computation | async-start | bytes 2621440 | tf_op jit(solution)/shard_map/all_to_all | solution.py:95
  76.1 1125.7 %reduce-scatter.5.cloned.1.call-start = ((), (), s32[]{:S(2)}) async-start(), calls=%async_computation.8 | async-start | bytes 1064960 | tf_op jit(solution)/shard_map/reduce_scatter | solution.py:168
  458.1 31.3 %collective-permute-start = (bf16[512,256]{1,0:T(8,128)(2,1)S(1)}, bf16[512,256]{1,0:T(8,128)(2,1)S(1)}, u32[]{:S(2)}, u32[]{:S(2)}) collective-permute-start(bf16[512,256]{1,0:T(8,128)(2,1)S(1)} %bitcast.75), channel_id=1, source_target_pairs={{0,4},{4,8},{8,12},{12,16},{16,20},{20,24},{24,28},{28,32},{32,36}... | collective-permute-start | bytes 786440 | tf_op jit(solution)/shard_map/ppermute | solution.py:15
  462.0 27.4 %collective-permute-start.1 = (bf16[512,256]{1,0:T(8,128)(2,1)S(1)}, bf16[512,256]{1,0:T(8,128)(2,1)}, u32[]{:S(2)}, u32[]{:S(2)}) collective-permute-start(bf16[512,256]{1,0:T(8,128)(2,1)S(1)} %bitcast.77), channel_id=1, source_target_pairs={{0,4},{4,8},{8,12},{12,16},{16,20},{20,24},{24,28},{28,32},{32,36}... | collective-permute-start | bytes 786440 | tf_op jit(solution)/shard_map/ppermute | solution.py:15
  485.6 1.5 copy-start.6
  560.7 1.7 copy-start
  631.8 4.7 copy-start.2
  631.8 4.7 copy-start.4
  775.2 1.0 copy-start.1
  775.2 791.0 %reduce-scatter.3.cloned.1.call-start = ((), (), s32[]{:S(2)}) async-start(), calls=%async_computation.7 | async-start | bytes 1064960 | tf_op jit(solution)/shard_map/reduce_scatter | solution.py:167
  776.2 8.3 collective-permute-start.3
  777.6 9.7 collective-permute-start.2
  778.9 5.6 copy-start.5
  781.9 5.4 copy-start.3
Sparse Core Ops, SparseCore 0:
  775.3 426.4 reduce-scatter.4
  1204.3 361.9 reduce-scatter.2
where the time goes:
time: 1590 us; the launch traced here: 1570 us
  waiting for transfers between devices  814 us (51%)
  blocking collectives  382 us (24%)
  matrix products  216 us (14%)
  local copies, waits for them, and re-layouts  72.1 us (5%)
  starting transfers between devices  36.3 us (2%)
  other arithmetic  30.7 us (2%)
    reduce_scatter x1, waiting for transfers between devices, shards(): lax.psum_scatter(pvalue_acc, 'ctx', scatter_dimension=0, tiled=True)  414 us
    reduce_scatter x1, waiting for transfers between devices, shards(): lax.psum_scatter(pkey_acc, 'ctx', scatter_dimension=0, tiled=True)  363 us
    all_gather x1, blocking collectives, shards(): lax.all_gather(prefix_keys, 'ctx', axis=0, tiled=True)  195 us
    all_gather x1, blocking collectives, shards(): lax.all_gather(prefix_values, 'ctx', axis=0, tiled=True)  187 us
    dot_general x40, matrix products, one_head(): logits = jnp.dot(query_h, key_h.T, preferred_element_type=jnp.float32)  48.4 us
    dot_general x40, matrix products, one_head(): jnp.dot(weights_b.T, grad_h, preferred_element_type=jnp.float32)  48.2 us
    dot_general x40, matrix products, one_head(): key_term = jnp.dot(dlogits.T, query_h, preferred_element_type=jnp.float32)  47.9 us
    dot_general x40, matrix products, one_head(): dweights = jnp.dot(grad_h, value_h.T, preferred_element_type=jnp.float32)  47.1 us
  transfers between devices with their start and end apart: 11, of which 8 were waited for; matrix products, arithmetic and copies ran while one was open for 2% of the time, Pallas kernels for 0%

commit v1 on v0

--- a/solution.py
+++ b/solution.py
@@ -130,8 +130,20 @@
         shifted(key_two.astype(jnp.bfloat16), "ctx", -1).astype(key_two.dtype),
         shifted(value_two.astype(jnp.bfloat16), "ctx", -1).astype(value_two.dtype),
     )
+
+    def part_forms_over_axis(mine_x, ax_name):
+        return jnp.concatenate(
+            jax.lax.all_to_all(
+                jnp.stack([mine_x] * jax.lax.psum(1, axis_name=ax_name)),
+                axis_name=ax_name,
+                concat_axis=0,
+                split_axis=0,
+            ),
+            0,
+        )
+
     whole_keys, whole_values = (
-        lax.all_gather(prefix_keys, "ctx", axis=0, tiled=True),
+        part_forms_over_axis(prefix_keys, "ctx"),
         lax.all_gather(prefix_values, "ctx", axis=0, tiled=True),
     )
     prompt_total = whole_keys.shape[0]

time: 1590 us -> 1410 us (0.89)
  blocking collectives: 382 us -> 195 us
    all_gather x1 -> x0, blocking collectives: 195 us -> none  [shards(): lax.all_gather(prefix_keys, 'ctx', axis=0, tiled=True)]
  transfers between devices with their start and end apart: 11 -> 12, of which waited for: 8 -> 8; matrix products, arithmetic and copies ran while one was open for 2% -> 13% of each run, Pallas kernels for 0% -> 0%
where the time goes in v1:
time: 1410 us; the launch traced here: 1400 us
  waiting for transfers between devices  819 us (58%)
  matrix products  217 us (15%)
  blocking collectives  195 us (14%)
  local copies, waits for them, and re-layouts  73.7 us (5%)
  starting transfers between devices  44.4 us (3%)
  other arithmetic  30.7 us (2%)
  between operations  14.3 us (1%)
    reduce_scatter x1, waiting for transfers between devices, shards(): lax.psum_scatter(pvalue_acc, 'ctx', scatter_dimension=0, tiled=True)  418 us
    reduce_scatter x1, waiting for transfers between devices, shards(): lax.psum_scatter(pkey_acc, 'ctx', scatter_dimension=0, tiled=True)  363 us
    all_gather x1, blocking collectives, shards(): lax.all_gather(prefix_values, 'ctx', axis=0, tiled=True)  195 us
    dot_general x40, matrix products, one_head(): logits = jnp.dot(query_h, key_h.T, preferred_element_type=jnp.float32)  49.1 us
    dot_general x40, matrix products, one_head(): jnp.dot(weights_b.T, grad_h, preferred_element_type=jnp.float32)  48.2 us
    dot_general x40, matrix products, one_head(): key_term = jnp.dot(dlogits.T, query_h, preferred_element_type=jnp.float32)  47.9 us
    dot_general x40, matrix products, one_head(): dweights = jnp.dot(grad_h, value_h.T, preferred_element_type=jnp.float32)  47.5 us
    dynamic_slice x40, local copies, waits for them, and re-layouts, one_head(): delta_h = lax.dynamic_slice_in_dim(deltas, head, 1, 1)  29.9 us
  transfers between devices with their start and end apart: 12, of which 8 were waited for; matrix products, arithmetic and copies ran while one was open for 13% of the time, Pallas kernels for 0%

profile of v1, /device:TPU:8, one launch (start us, length us, event | category | flops | bytes accessed | tf_op | source)
XLA Modules:
  0.0 1403.0 jit_solution(4384013542308841072)
XLA Ops:
  8.9 5.5 all-to-all-start.1
  16.2 2.7 all-to-all-done.1
  18.9 5.0 all-to-all-start.3
  25.3 2.9 all-to-all-done.3
  28.2 5.3 all-to-all-start.2
  35.0 14.2 %all-to-all-done.2 = bf16[128,4,1280]{0,2,1:T(8,128)(2,1)S(1)} async-done(((bf16[128,4,1280]{0,2,1:T(8,128)(2,1)}), bf16[128,4,1280]{0,2,1:T(8,128)(2,1)S(1)}, u32[]{:S(2)}, u32[]{:S(2)}) %all-to-all-start.2) | async-done | bytes 1310752 | tf_op jit(solution)/shard_map/all_to_all | solution.py:99
  49.1 5.3 all-to-all-start.4
  54.8 2.5 copy.65
  57.6 12.4 all-to-all-done.4
  70.0 6.1 all-to-all-start
  76.4 195.1 %all_gather.3 = bf16[1024,256]{1,0:T(8,128)(2,1)} all-gather(bf16[16,256]{1,0:T(8,128)(2,1)S(1)} %copy-done.13), channel_id=1, replica_groups=mesh['ctx'=64,'head'=4] {'ctx'}, dimensions={0}, use_global_device_ids=true | all-gather | bytes 532480 | tf_op jit(solution)/shard_map/all_gather | solution.py:147
  275.0 6.9 copy.49
  282.0 3.5 reshape.106
  285.4 6.9 copy.51
  292.3 3.5 reshape.107
  297.3 2.3 fusion.69
  300.4 11.0 all-to-all-start.5
  314.2 70.8 %while.79 = (s32[]{:T(128)}, f32[512,1280]{1,0:T(8,128)}, f32[512,256]{1,0:T(8,128)S(1)}, f32[512,256]{1,0:T(8,128)S(1)}, bf16[512,1280]{1,0:T(8,128)(2,1)}, /*i...) while((s32[]{:T(128)}, f32[512,1280]{1,0:T(8,128)}, ...), condition=%wide.region_5.6_spmd.clone, body=%wide.region_4.5_spmd.clone.sunk | while | flops 337772544 | bytes 8012191 | solution.py:74
  386.8 69.1 %while.78 = (s32[]{:T(128)}, f32[512,1280]{1,0:T(8,128)}, f32[512,256]{1,0:T(8,128)S(1)}, f32[512,256]{1,0:T(8,128)S(1)}, bf16[512,1280]{1,0:T(8,128)(2,1)}, /*i...) while((s32[]{:T(128)}, f32[512,1280]{1,0:T(8,128)}, ...), condition=%wide.region_3.4_spmd.clone, body=%wide.region_2.3_spmd.clone.sunk | while | flops 338296832 | bytes 6961531 | solution.py:74
  455.9 4.7 add.320
  462.7 136.6 %while.80 = (s32[]{:T(128)}, f32[512,1280]{1,0:T(8,128)}, f32[1024,256]{1,0:T(8,128)}, f32[1024,256]{1,0:T(8,128)}, bf16[1024,256]{1,0:T(8,128)(2,1)}, /*index=5...) while((s32[]{:T(128)}, f32[512,1280]{1,0:T(8,128)}, ...), condition=%wide.region_15.16_spmd.clone, body=%wide.region_9.15_spmd.clone.sunk | while | flops 85099536 | bytes 14145448 | solution.py:177
  464.1 62.4 %conditional.3 = ((f32[512,1280]{1,0:T(8,128)}, f32[1024,256]{1,0:T(8,128)}, f32[1024,256]{1,0:T(8,128)})) conditional(s32[]{:T(128)} %convert_element_type.143, (f32[512,1280]{1,0:T(8,128)}, f32[1024,256]{1,0:T(8,128)}, f32[1024,256]{1,0:T(8,128)}) %tuple.159, (s32[]{:T(128)}, bf16[1024,256]{1,0:T(8,128)(2,1)}, bf16[1024,256]{1,0:T(8,128)(2,1)}, ...), branch_computations={%region_11.11_spmd, %region_12.14_spmd} | conditional | flops 85098512 | bytes 14136441 | solution.py:175
  466.1 55.2 %while.77 = (s32[]{:T(128)}, f32[512,1280]{1,0:T(8,128)S(1)}, f32[128,256]{1,0:T(8,128)S(1)}, f32[128,256]{1,0:T(8,128)S(1)}, bf16[512,1280]{1,0:T(8,128)(2,1)},...) while((s32[]{:T(128)}, f32[512,1280]{1,0:T(8,128)S(1)}, ...), condition=%wide.region_14.13_spmd.clone, body=%wide.region_13.12_spmd.clone.sunk | while | flops 84377616 | bytes 2339707 | solution.py:74
  523.0 3.5 add.309
  535.4 62.4 %conditional.3 = ((f32[512,1280]{1,0:T(8,128)}, f32[1024,256]{1,0:T(8,128)}, f32[1024,256]{1,0:T(8,128)})) conditional(s32[]{:T(128)} %convert_element_type.143, (f32[512,1280]{1,0:T(8,128)}, f32[1024,256]{1,0:T(8,128)}, f32[1024,256]{1,0:T(8,128)}) %tuple.159, (s32[]{:T(128)}, bf16[1024,256]{1,0:T(8,128)(2,1)}, bf16[1024,256]{1,0:T(8,128)(2,1)}, ...), branch_computations={%region_11.11_spmd, %region_12.14_spmd} | conditional | flops 85098512 | bytes 14136441 | solution.py:175
  537.3 55.2 %while.77 = (s32[]{:T(128)}, f32[512,1280]{1,0:T(8,128)S(1)}, f32[128,256]{1,0:T(8,128)S(1)}, f32[128,256]{1,0:T(8,128)S(1)}, bf16[512,1280]{1,0:T(8,128)(2,1)},...) while((s32[]{:T(128)}, f32[512,1280]{1,0:T(8,128)S(1)}, ...), condition=%wide.region_14.13_spmd.clone, body=%wide.region_13.12_spmd.clone.sunk | while | flops 84377616 | bytes 2339707 | solution.py:74
  594.2 3.5 add.309
  603.0 3.1 multiply_convert_fusion
  606.0 2.6 collective-permute-done.3
  609.4 2.0 collective-permute-done.2
  612.2 418.1 %reduce-scatter.5.cloned.1.call-done = f32[16,256]{1,0:T(8,128)} async-done(((f32[1024,256]{1,0:T(8,128)}), f32[16,256]{1,0:T(8,128)}) %reduce-scatter.5.cloned.1.call-update) | async-done | bytes 16400 | tf_op jit(solution)/shard_map/reduce_scatter | solution.py:180
  1031.6 363.2 %reduce-scatter.3.cloned.1.call-done = f32[16,256]{1,0:T(8,128)} async-done(((f32[1024,256]{1,0:T(8,128)}), f32[16,256]{1,0:T(8,128)}) %reduce-scatter.3.cloned.1.call-update) | async-done | bytes 16400 | tf_op jit(solution)/shard_map/reduce_scatter | solution.py:179
  (381 shorter events, 288.0 us)
Async XLA Ops:
  7.2 16.7 %copy-start.11 = (bf16[128,5120]{1,0:T(8,128)(2,1)S(1)}, bf16[128,5120]{1,0:T(8,128)(2,1)}, u32[]{:S(2)}) copy-start(bf16[128,5120]{1,0:T(8,128)(2,1)} %param.24) | copy-start | bytes 3932164
  8.9 9.9 all-to-all-start.1
  18.9 9.4 all-to-all-start.3
  28.2 244.6 %copy-start.7 = (bf16[128,4,256]{2,0,1:T(8,128)(2,1)}, bf16[128,4,256]{2,0,1:T(8,128)(2,1)S(1)}, u32[]{:S(2)}) copy-start(bf16[128,4,256]{2,0,1:T(8,128)(2,1)S(1)} %all-to-all-done.3) | copy-start | bytes 786436
  28.2 5.3 copy-start.12
  28.2 20.9 %all-to-all-start.2 = ((bf16[128,4,1280]{0,2,1:T(8,128)(2,1)}), bf16[128,4,1280]{0,2,1:T(8,128)(2,1)S(1)}, u32[]{:S(2)}, u32[]{:S(2)}) async-start(bf16[128,4,1280]{0,2,1:T(8,128)(2,1)} %bitcast.5), calls=%async_computation.2 | async-start | bytes 2621440 | tf_op jit(solution)/shard_map/all_to_all | solution.py:99
  49.1 5.3 copy-start.16
  49.1 20.9 %all-to-all-start.4 = ((bf16[128,4,1280]{0,2,1:T(8,128)(2,1)}), bf16[128,4,1280]{0,2,1:T(8,128)(2,1)S(1)}, u32[]{:S(2)}, u32[]{:S(2)}) async-start(bf16[128,4,1280]{0,2,1:T(8,128)(2,1)} %bitcast.74), calls=%async_computation.4 | async-start | bytes 2621440 | tf_op jit(solution)/shard_map/all_to_all | solution.py:98
  54.8 2.5 copy-start.15
  70.0 6.4 copy-start.13
  70.0 229.6 %all-to-all-start = ((bf16[128,4,1280]{2,0,1:T(8,128)(2,1)}), bf16[128,4,1280]{2,0,1:T(8,128)(2,1)}, u32[]{:S(2)}, u32[]{:S(2)}) async-start(bf16[128,4,1280]{2,0,1:T(8,128)(2,1)} %bitcast.73), calls=%async_computation | async-start | bytes 2621440 | tf_op jit(solution)/shard_map/all_to_all | solution.py:95
  271.6 40.1 %collective-permute-start = (bf16[512,256]{1,0:T(8,128)(2,1)S(1)}, bf16[512,256]{1,0:T(8,128)(2,1)S(1)}, u32[]{:S(2)}, u32[]{:S(2)}) collective-permute-start(bf16[512,256]{1,0:T(8,128)(2,1)S(1)} %bitcast.76), channel_id=1, source_target_pairs={{0,4},{4,8},{8,12},{12,16},{16,20},{20,24},{24,28},{28,32},{32,36}... | collective-permute-start | bytes 786440 | tf_op jit(solution)/shard_map/ppermute | solution.py:15
  272.9 38.8 %collective-permute-start.1 = (bf16[512,256]{1,0:T(8,128)(2,1)S(1)}, bf16[512,256]{1,0:T(8,128)(2,1)}, u32[]{:S(2)}, u32[]{:S(2)}) collective-permute-start(bf16[512,256]{1,0:T(8,128)(2,1)S(1)} %bitcast.78), channel_id=1, source_target_pairs={{0,4},{4,8},{8,12},{12,16},{16,20},{20,24},{24,28},{28,32},{32,36}... | collective-permute-start | bytes 786440 | tf_op jit(solution)/shard_map/ppermute | solution.py:15
  295.8 1.5 copy-start.6
  297.3 2.3 copy-start.14
  300.4 160.2 %all-to-all-start.5 = ((bf16[64,16,256]{2,1,0:T(8,128)(2,1)}), bf16[64,16,256]{2,1,0:T(8,128)(2,1)}, u32[]{:S(2)}, u32[]{:S(2)}) async-start(bf16[64,16,256]{2,1,0:T(8,128)(2,1)} %stack.2), calls=%async_computation.5 | async-start | bytes 1048576 | tf_op jit(solution)/shard_map/all_to_all | solution.py:136
  311.5 718.9 %reduce-scatter.5.cloned.1.call-start = ((), (), s32[]{:S(2)}) async-start(), calls=%async_computation.9 | async-start | bytes 1064960 | tf_op jit(solution)/shard_map/reduce_scatter | solution.py:180
  316.4 1.3 copy-start.10
  323.4 1.3 copy-start.10
  330.5 1.3 copy-start.10
  337.6 1.3 copy-start.10
  351.7 1.3 copy-start.10
  373.0 1.3 copy-start.10
  385.0 1.7 copy-start
  385.0 1.8 copy-start.8
  455.9 4.7 copy-start.2
  455.9 4.7 copy-start.4
  599.3 795.5 %reduce-scatter.3.cloned.1.call-start = ((), (), s32[]{:S(2)}) async-start(), calls=%async_computation.8 | async-start | bytes 1064960 | tf_op jit(solution)/shard_map/reduce_scatter | solution.py:179
  600.3 8.3 collective-permute-start.3
  601.7 9.7 collective-permute-start.2
  603.0 5.6 copy-start.5
  606.0 5.4 copy-start.3
  (6 other events, 7.1 us)
Sparse Core Ops, SparseCore 0:
  599.4 430.8 reduce-scatter.4
  1032.8 361.9 reduce-scatter.2
